TPU v7x, 512 devices: a whole 4x4x16 slice. The times are simulated.
512 devices in a mesh: pipe: 16 (over z_hi, y), zero: 32 (over z_lo, x, core).
Axes of the slice: x: 4, y: 4, z: 16 (z_hi: 4, z_lo: 4; z = z_hi * 4 + z_lo), core: 2. Of those that a mesh axis runs over, the one named last changes fastest.
Arguments:
- residual: bfloat16 [16, 2048, 4096], P('pipe', 'zero'), may hold values from -6 to 6
- norm_gain: bfloat16 [16, 4096], P('pipe'), may hold values from 0.099609375 to 1.8984375
- queries: bfloat16 [16, 2048, 4096], P('pipe', 'zero'), may hold values from -74 to 74
- cached_kv: bfloat16 [16, 512, 1024], P('pipe', 'zero'), may hold values from -6 to 6
- panel_blocks: bfloat16 [16, 160, 128, 128], P('pipe', 'zero'), may hold values from -0.125 to 0.125
- block_rows: int32 [16, 8, 20], P('pipe'), may hold values from 0 to 31, as said below
- counts: int32 [16, 8], P('pipe'), may hold values from 12 to 20, as said below
Outputs:
- passed: bfloat16 [16, 2048, 4096], P('pipe', 'zero')
- new_kv: bfloat16 [16, 2048, 1024], P('pipe', 'zero')
Inputs may be any that keep to these rules, and one draw needn't show every extreme that they name: `block_rows`: row blocks named by the slots of one panel are all different. `counts`: slots at or beyond a panel's count are padding.
All inputs are finite; a program needn't handle non-finite values.
Results may differ from a plain program's by a relative error of at most 0.0047.
The roundings to bfloat16 on the way count: a program that leaves them out, or rounds other values in their place, can miss the bound.
Values may be sent and summed in bfloat16 or wider, within the bound.
No kernel may reach another device: no remote copies, remote signals or barrier semaphores. Data moves between devices by JAX's collectives and lax.ppermute only.
A program may use at most 64 MiB of HBM per device.

v0:
```python
import math
import jax
import jax.numpy as jnp
from jax import lax
from jax.sharding import PartitionSpec as P

QH = 32
KVH = 4
HD = 128


def passed_along(block, axis, distance):
    devices = range(lax.axis_size(axis))
    route = [((i - distance) % len(devices), i) for i in devices]
    return lax.ppermute(block, axis, route)


def local(residual, norm_gain, queries, cached_kv, panel_blocks, block_rows, counts):
    row_count = residual.shape[1]
    model_width = residual.shape[2]
    zero_index = lax.axis_index("zero")
    stream = residual[0].astype(jnp.float32)
    normed = (
        stream
        * lax.rsqrt(jnp.mean(stream * stream, axis=-1, keepdims=True) + 1e-05)
        * norm_gain[0].astype(jnp.float32)
    ).astype(jnp.bfloat16)
    block_size = panel_blocks.shape[-1]
    panels = block_rows.shape[1]
    slot_depth = block_rows.shape[2]
    row_table = block_rows[0].reshape(-1)
    slot_live = (
        (jnp.arange(slot_depth)[None, :] < counts[0][:, None]).astype(jnp.float32).reshape(-1)
    )
    normed_grid = normed.reshape(row_count, model_width // block_size, block_size)
    kv_heads = KVH
    head_size = HD
    group_size = QH // KVH
    kv_width = kv_heads * head_size
    score_scale = 1.0 / math.sqrt(head_size)
    query_grid = queries[0].reshape(row_count, kv_heads, group_size, head_size)
    first_query = zero_index * row_count
    query_pos = first_query + jnp.arange(row_count)
    initial = (
        jnp.full((kv_heads, row_count, group_size), -1e30, jnp.float32),
        jnp.zeros((kv_heads, row_count, group_size), jnp.float32),
        jnp.zeros((kv_heads, row_count, group_size, head_size), jnp.float32),
    )

    def absorb(running, portion, visible):
        run_max, run_sum, run_acc = running
        key_count = portion.shape[0]
        key_grid = portion[:, :kv_width].reshape(key_count, kv_heads, head_size)
        value_grid = portion[:, kv_width:].reshape(key_count, kv_heads, head_size)
        scores = (
            jnp.einsum("rgjd,ngd->grjn", query_grid, key_grid, preferred_element_type=jnp.float32)
            * score_scale
        )
        visible_mask = visible[None, :, None, :]
        new_max = jnp.maximum(run_max, jnp.max(jnp.where(visible_mask, scores, -1e30), axis=-1))
        shrink = jnp.exp(run_max - new_max)
        weights = jnp.where(visible_mask, jnp.exp(scores - new_max[..., None]), 0.0)
        new_sum = run_sum * shrink + jnp.sum(weights, axis=-1)
        new_acc = run_acc * shrink[..., None] + jnp.einsum(
            "grjn,ngd->grjd",
            weights.astype(jnp.bfloat16),
            value_grid,
            preferred_element_type=jnp.float32,
        )
        return (new_max, new_sum, new_acc)

    chosen = jnp.take(normed_grid, row_table, axis=1)
    slot_terms = jnp.einsum(
        "rsk,skn->rsn",
        chosen,
        lax.all_gather(panel_blocks[0], "zero", axis=0, tiled=True),
        preferred_element_type=jnp.float32,
    )
    slot_terms = slot_terms * slot_live[None, :, None]
    summed = slot_terms.reshape(row_count, panels, slot_depth, block_size).sum(axis=2)
    kv_new = summed.reshape(row_count, panels * block_size).astype(jnp.bfloat16)
    cache_portion = lax.all_gather(cached_kv[0], "zero", axis=0, tiled=True)
    softmax_state = absorb(
        initial, cache_portion, jnp.ones((row_count, cache_portion.shape[0]), bool)
    )
    portion = lax.all_gather(kv_new, "zero", axis=0, tiled=True)
    key_pos = jnp.arange(portion.shape[0])
    visible = key_pos[None, :] <= query_pos[:, None]
    softmax_state = lax.cond(
        jnp.int32(0) <= first_query + row_count - 1,
        lambda state_in: absorb(state_in, portion, visible),
        lambda state_in: state_in,
        softmax_state,
    )
    run_max, denominator, run_acc = softmax_state
    attended = run_acc / denominator[..., None]
    attended = jnp.transpose(attended, (1, 0, 2, 3)).reshape(
        row_count, kv_heads * group_size * head_size
    )
    updated = (stream + attended).astype(jnp.bfloat16)
    passed = passed_along(updated[None], "pipe", 1)
    return (passed, kv_new[None])


def solution(mesh):
    in_specs = (
        P("pipe", "zero", None),
        P("pipe", None),
        P("pipe", "zero", None),
        P("pipe", "zero", None),
        P("pipe", "zero", None, None),
        P("pipe", None, None),
        P("pipe", None),
    )
    out_specs = (P("pipe", "zero", None), P("pipe", "zero", None))
    return jax.shard_map(local, mesh=mesh, in_specs=in_specs, out_specs=out_specs, check_vma=False)
```

profile of v0, /device:TPU:96, one launch (start us, length us, event | category | flops | bytes accessed | tf_op | source)
XLA Modules:
  0.0 306.2 jit_solution(14598807501692515659)
XLA Ops:
  7.2 0.0 copy-start
  7.2 0.0 all-gather.10.cloned.1.call-start
  7.2 0.7 all-gather.10.cloned.1.call-update
  7.9 0.0 all-gather.8.cloned.1.call-start
  8.0 0.7 all-gather.8.cloned.1.call-update
  8.7 0.0 all-gather.6.cloned.1.call-start
  8.7 1.1 convert_bitcast_fusion
  9.8 0.7 fusion.37
  10.6 0.8 reshape_squeeze.10
  11.3 0.8 reshape_squeeze.9
  12.1 0.1 reshape.131
  12.2 0.7 mul.79
  12.9 0.2 copy.67
  13.1 0.0 copy-done
  13.1 0.2 fusion.31
  13.4 0.7 fusion.34
  14.1 1.1 gather_fusion
  15.1 66.1 %all-gather.10.cloned.1.call-done = bf16[1,160,128,128]{3,2,0,1:T(8,128)(2,1)} async-done(((bf16[1,5,128,128]{3,2,0,1:T(8,128)(2,1)}), bf16[1,160,128,128]{3,2,0,1:T(8,128)(2,1)}) %all-gather.10.cloned.1.call-update) | async-done | bytes 5242896 | tf_op jit(solution)/shard_map/all_gather | solution.py:76
  81.3 6.4 %broadcast_multiply_fusion = f32[160,64,128]{2,1,0:T(8,128)} fusion(f32[160]{0:T(256)S(1)} %reshape.131, bf16[1,160,128,128]{3,2,0,1:T(8,128)(2,1)} %all-gather.10.cloned.1.call-done, bf16[160,64,128]{2,1,0:T(8,128)(2,1)S(1)} %gather_fusion, pred[160]{0:T(512)(128)(4,1)S(1)} %compare_and_fusion), kind=kOutput, calls=%fused_computation.24 | convolution fusion | flops 338165760 | bytes 13108000 | tf_op jit(solution)/shard_map/rsk,skn->rsn/dot_general | solution.py:73
  87.7 0.0 copy-start.2
  87.7 3.0 reduce_sum.38
  90.7 0.7 copy_bitcast_fusion
  91.4 0.0 all-gather.6.cloned.1.call-update
  91.4 0.0 copy-done.2
  91.4 0.1 copy.66
  91.5 54.7 %all-gather.8.cloned.1.call-done = bf16[1,512,1024]{2,1,0:T(8,128)(2,1)} async-done(((bf16[1,16,1024]{2,1,0:T(8,128)(2,1)}), bf16[1,512,1024]{2,1,0:T(8,128)(2,1)}) %all-gather.8.cloned.1.call-update) | async-done | bytes 1048592 | tf_op jit(solution)/shard_map/all_gather | solution.py:82
  146.2 1.5 copy.42
  147.7 0.1 fusion.42
  147.7 0.8 multiply_reduce_fusion
  148.5 1.3 fusion.15
  149.9 1.5 fusion.27
  151.3 64.2 %all-gather.6.cloned.1.call-done = bf16[2048,1024]{1,0:T(8,128)(2,1)} async-done(((bf16[64,1024]{1,0:T(8,128)(2,1)}), bf16[2048,1024]{1,0:T(8,128)(2,1)}) %all-gather.6.cloned.1.call-update) | async-done | bytes 4194320 | tf_op jit(solution)/shard_map/all_gather | solution.py:86
  215.6 26.3 %conditional.1 = ((f32[4,64,8]{2,1,0:T(8,128)S(1)}, f32[4,64,8,128]{3,2,1,0:T(8,128)S(1)})) conditional(s32[]{:T(128)} %convert_element_type.57, (f32[4,64,8]{2,1,0:T(8,128)S(1)}, f32[4,64,8,128]{3,2,1,0:T(8,128)S(1)}) %tuple.15, (s32[]{:T(128)}, s32[64,1]{0,1:T(1,128)S(1)}, s32[64,2048]{1,0:T(8,128)S(1)}, bf16[2048,1024]{1,0:T(8,128)(2,1)}, ...), branch_computations={%region_4.5_spmd, %region_5.8_spmd} | conditional | flops 2194280448 | bytes 75088664 | solution.py:89
  215.6 0.1 broadcast_compare_fusion
  215.8 6.5 %copy.49 = bf16[2048,1024]{0,1:T(8,128)(2,1)} copy(bf16[2048,1024]{1,0:T(8,128)(2,1)} %get-tuple-element.66) | data formatting | bytes 8388608 | tf_op jit(solution)/shard_map
  222.3 4.0 %fusion.41 = (bf16[2048,512]{0,1:T(8,128)(2,1)}, bf16[2048,512]{0,1:T(8,128)(2,1)S(1)}) fusion(bf16[2048,1024]{0,1:T(8,128)(2,1)} %copy.49), kind=kLoop, calls=%fused_computation.55 | loop fusion | bytes 8388608 | tf_op jit(solution)/shard_map/cond/branch_1_fun/slice | solution.py:54
  226.3 3.9 %select_reduce_fusion = (f32[4,64,8]{2,1,0:T(8,128)S(1)}, f32[4,64,8,2048]{3,2,1,0:T(8,128)S(1)}) fusion(pred[64,2048]{1,0:T(8,128)(4,1)S(1)} %broadcast_compare_fusion, bf16[2048,4,128,1]{0,2,3,1:T(8,128)(2,1)S(1)} %bitcast.62, bf16[64,4,8,128]{3,2,1,0:T(8,128)(2,1)S(1)} %get-tuple-element.67), kind=kOutput, calls=%fused_computation.2 | convolution fusion | flops 1086322688 | bytes 19537920 | tf_op jit(solution)/shard_map/cond/branch_1_fun/rgjd,ngd->grjn/dot_general | solution.py:56
  230.2 5.0 %fusion.1 = f32[4,64,8]{2,1,0:T(8,128)S(1)} fusion(f32[4,64,8,2048]{3,2,1,0:T(8,128)S(1)} %get-tuple-element.76, f32[4,64,8]{2,1,0:T(8,128)S(1)} %max.2, pred[64,2048]{1,0:T(8,128)(4,1)S(1)} %broadcast_compare_fusion), kind=kLoop, calls=%fused_computation.4 | loop fusion | flops 16775168 | bytes 16924672 | tf_op jit(solution)/shard_map/cond/branch_1_fun/reduce_sum | solution.py:63
  235.2 0.1 multiply_add_fusion
  235.3 6.5 %fusion.5 = f32[4,64,8,128]{3,2,1,0:T(8,128)S(1)} fusion(bf16[2048,4,128,1]{0,2,3,1:T(8,128)(2,1)} %bitcast.68, f32[4,64,8,2048]{3,2,1,0:T(8,128)S(1)} %get-tuple-element.76, f32[4,64,8]{2,1,0:T(8,128)S(1)} %max.2, pred[64,2048]{1,0:T(8,128)(4,1)S(1)} %broadcast_compare_fusion, f32[4,64,8,128]{3,2,1,0:T(8,128)S(1)} %get-tuple-element.32, ...), kind=kOutput, calls=%fused_computation.7 | convolution fusion | flops 1091043328 | bytes 21118976 | tf_op jit(solution)/shard_map/cond/branch_1_fun/grjn,ngd->grjd/dot_general | solution.py:64
  241.9 0.0 copy-start.1
  241.9 0.3 divide_bitcast_fusion
  242.2 0.1 copy.51
  242.4 0.2 reshape.128
  242.6 0.3 copy-done.1
  242.9 0.1 fusion.32
  243.0 3.4 %collective-permute-start = (bf16[1,64,4096]{2,1,0:T(8,128)(2,1)S(1)}, bf16[1,64,4096]{2,1,0:T(8,128)(2,1)S(1)}, u32[]{:S(2)}, u32[]{:S(2)}) collective-permute-start(bf16[1,64,4096]{2,1,0:T(8,128)(2,1)S(1)} %fusion.32), channel_id=1, source_target_pairs={{480,0},{0,32},{32,64},{64,96},{96,128},{128,160},{160,192},{192,2... | collective-permute-start | bytes 1572872 | tf_op jit(solution)/shard_map/ppermute | solution.py:15
  246.4 0.1 copy.48
  246.5 0.7 convert_element_type.67
  247.2 51.6 %collective-permute-done = bf16[1,64,4096]{2,1,0:T(8,128)(2,1)S(1)} collective-permute-done((bf16[1,64,4096]{2,1,0:T(8,128)(2,1)S(1)}, bf16[1,64,4096]{2,1,0:T(8,128)(2,1)S(1)}, u32[]{:S(2)}, u32[]{:S(2)}) %collective-permute-start) | collective-permute-done | bytes 524320 | tf_op jit(solution)/shard_map/ppermute | solution.py:15
  298.9 0.8 copy.87
  (10 shorter events, 0.1 us)
Async XLA Ops:
  7.2 6.0 %copy-start = (bf16[1,64,4096]{2,1,0:T(8,128)(2,1)S(1)}, bf16[1,64,4096]{2,1,0:T(8,128)(2,1)}, u32[]{:S(2)}) copy-start(bf16[1,64,4096]{2,1,0:T(8,128)(2,1)} %param.9) | copy-start | bytes 1572868
  7.2 74.1 %all-gather.10.cloned.1.call-start = ((), (), s32[]{:S(2)}) async-start(), calls=%async_computation.2 | async-start | bytes 5406720 | tf_op jit(solution)/shard_map/all_gather | solution.py:76
  7.9 138.3 %all-gather.8.cloned.1.call-start = ((), (), s32[]{:S(2)}) async-start(), calls=%async_computation.1 | async-start | bytes 1081344 | tf_op jit(solution)/shard_map/all_gather | solution.py:82
  8.7 206.9 %all-gather.6.cloned.1.call-start = ((), (), s32[]{:S(2)}) async-start(), calls=%async_computation | async-start | bytes 4325376 | tf_op jit(solution)/shard_map/all_gather | solution.py:86
  87.7 3.7 %copy-start.2 = (bf16[1,64,4096]{2,1,0:T(8,128)(2,1)S(1)}, bf16[1,64,4096]{2,1,0:T(8,128)(2,1)}, u32[]{:S(2)}) copy-start(bf16[1,64,4096]{2,1,0:T(8,128)(2,1)} %param.11) | copy-start | bytes 1572868
  241.9 1.0 copy-start.1
  243.0 55.8 %collective-permute-start = (bf16[1,64,4096]{2,1,0:T(8,128)(2,1)S(1)}, bf16[1,64,4096]{2,1,0:T(8,128)(2,1)S(1)}, u32[]{:S(2)}, u32[]{:S(2)}) collective-permute-start(bf16[1,64,4096]{2,1,0:T(8,128)(2,1)S(1)} %fusion.32), channel_id=1, source_target_pairs={{480,0},{0,32},{32,64},{64,96},{96,128},{128,160},{160,192},{192,2... | collective-permute-start | bytes 1572872 | tf_op jit(solution)/shard_map/ppermute | solution.py:15
Sparse Core Ops, SparseCore 0:
  10.1 71.0 all-gather.9
  83.4 62.7 all-gather.7
  148.9 66.6 all-gather.5
where the time goes:
time: 307 us; the launch traced here: 306 us
  waiting for transfers between devices  238 us (78%)
  matrix products  19 us (6%)
  local copies, waits for them, and re-layouts  18 us (6%)
  between operations  14 us (5%)
  other arithmetic  13.6 us (4%)
  starting transfers between devices  3.49 us (1%)
    all_gather x1, waiting for transfers between devices, local(): lax.all_gather(panel_blocks[0], 'zero', axis=0, tiled=True)  66.1 us
    all_gather x1, waiting for transfers between devices, local(): portion = lax.all_gather(kv_new, 'zero', axis=0, tiled=True)  64.2 us
    all_gather x1, waiting for transfers between devices, local(): cache_portion = lax.all_gather(cached_kv[0], 'zero', axis=0, tiled=True)  54.7 us
    ppermute x1, waiting for transfers between devices, passed_along(): return lax.ppermute(block, axis, route)  51.6 us
    dot_general x2, matrix products, absorb(): jnp.einsum('grjn,ngd->grjd', weights.astype(jnp.bfloat16), value_grid, pr...  8.01 us
    another operation x1, local copies, waits for them, and re-layouts  6.53 us
    dot_general x1, matrix products, local(): jnp.einsum('rsk,skn->rsn', chosen, lax.all_gather(panel_blocks[0], 'zero'...  6.4 us
    reduce_sum x2, other arithmetic, absorb(): new_sum = run_sum * shrink + jnp.sum(weights, axis=-1)  6.31 us
  transfers between devices with their start and end apart: 4, of which 4 were waited for; matrix products, arithmetic and copies ran while one was open for 7% of the time, Pallas kernels for 0%

commit v1 on v0

--- a/solution.py
+++ b/solution.py
@@ -79,7 +79,11 @@
     slot_terms = slot_terms * slot_live[None, :, None]
     summed = slot_terms.reshape(row_count, panels, slot_depth, block_size).sum(axis=2)
     kv_new = summed.reshape(row_count, panels * block_size).astype(jnp.bfloat16)
-    cache_portion = lax.all_gather(cached_kv[0], "zero", axis=0, tiled=True)
+    buf = cached_kv[0]
+    leaves = []
+    for _ in range(lax.axis_size("zero")):
+        leaves.append(buf)
+    cache_portion = jnp.concatenate(lax.all_to_all(jnp.stack(leaves, 0), "zero", 0, 0), 0)
     softmax_state = absorb(
         initial, cache_portion, jnp.ones((row_count, cache_portion.shape[0]), bool)
     )

time: 307 us -> 256 us (0.83)
  the two profiles are of different devices: /device:TPU:96 before, /device:TPU:67 now
where the time goes in v1:
time: 256 us
  waiting for transfers between devices  181 us (71%)
  matrix products  19 us (7%)
  local copies, waits for them, and re-layouts  18.1 us (7%)
  between operations  14.3 us (6%)
  other arithmetic  13.6 us (5%)
  starting transfers between devices  9.94 us (4%)
    all_gather x1, waiting for transfers between devices, local(): lax.all_gather(panel_blocks[0], 'zero', axis=0, tiled=True)  67.7 us
    ppermute x1, waiting for transfers between devices, passed_along(): return lax.ppermute(block, axis, route)  51.5 us
    all_gather x1, waiting for transfers between devices, local(): portion = lax.all_gather(kv_new, 'zero', axis=0, tiled=True)  31.7 us
    all_to_all x1, waiting for transfers between devices, local(): lax.all_to_all(jnp.stack(leaves, 0), 'zero', 0, 0)  29.1 us
    dot_general x2, matrix products, absorb(): jnp.einsum('grjn,ngd->grjd', weights.astype(jnp.bfloat16), value_grid, pr...  7.99 us
    all_to_all x1, starting transfers between devices, local(): lax.all_to_all(jnp.stack(leaves, 0), 'zero', 0, 0)  6.75 us
    another operation x1, local copies, waits for them, and re-layouts  6.53 us
    dot_general x1, matrix products, local(): jnp.einsum('rsk,skn->rsn', chosen, lax.all_gather(panel_blocks[0], 'zero'...  6.41 us
  transfers between devices with their start and end apart: 4, of which 4 were waited for; matrix products, arithmetic and copies ran while one was open for 5% of the time, Pallas kernels for 0%

profile of v1, /device:TPU:67, one launch (start us, length us, event | category | flops | bytes accessed | tf_op | source)
XLA Modules:
  0.0 255.7 jit_solution(1734121734246441163)
XLA Ops:
  7.2 0.0 copy-start
  7.2 0.0 all-gather.6.cloned.1.call-start
  7.2 0.7 all-gather.6.cloned.1.call-update
  7.9 0.0 all-gather.4.cloned.1.call-start
  8.0 0.8 reshape_squeeze.10
  8.7 0.8 reshape_squeeze.9
  9.5 0.7 fusion.37
  10.2 0.1 reshape.136
  10.3 0.7 mul.79
  11.0 1.1 convert_bitcast_fusion
  12.2 0.2 copy.70
  12.4 0.0 copy-done
  12.4 0.2 fusion.31
  12.6 0.7 fusion.34
  13.3 1.1 gather_fusion
  14.4 67.7 %all-gather.6.cloned.1.call-done = bf16[1,160,128,128]{3,2,0,1:T(8,128)(2,1)} async-done(((bf16[1,5,128,128]{3,2,0,1:T(8,128)(2,1)}), bf16[1,160,128,128]{3,2,0,1:T(8,128)(2,1)}) %all-gather.6.cloned.1.call-update) | async-done | bytes 5242896 | tf_op jit(solution)/shard_map/all_gather | solution.py:76
  82.1 6.4 %broadcast_multiply_fusion = f32[160,64,128]{2,1,0:T(8,128)} fusion(f32[160]{0:T(256)S(1)} %reshape.136, bf16[1,160,128,128]{3,2,0,1:T(8,128)(2,1)} %all-gather.6.cloned.1.call-done, bf16[160,64,128]{2,1,0:T(8,128)(2,1)S(1)} %gather_fusion, pred[160]{0:T(512)(128)(4,1)S(1)} %compare_and_fusion), kind=kOutput, calls=%fused_computation.24 | convolution fusion | flops 338165760 | bytes 13108000 | tf_op jit(solution)/shard_map/rsk,skn->rsn/dot_general | solution.py:73
  88.5 0.0 copy-start.5
  88.5 0.0 copy-start.4
  88.5 3.0 %reduce_sum.38 = bf16[64,8,128]{2,0,1:T(8,128)(2,1)S(1)} reduce(f32[64,8,20,128]{3,0,2,1:T(8,128)} %bitcast.62, f32[]{:T(128)} %constant.28.clone.1), dimensions={2}, to_apply=%region_3.4 | reduce | flops 1245184 | bytes 5373956 | tf_op jit(solution)/shard_map/reduce_sum | solution.py:80
  91.5 0.0 copy-start.2
  91.5 0.7 copy_bitcast_fusion
  92.2 0.0 all-gather.4.cloned.1.call-update
  92.2 0.0 copy-done.5
  92.2 1.1 stack.3
  93.3 6.8 %all-to-all-start = ((bf16[32,16,1024]{2,1,0:T(8,128)(2,1)}), bf16[32,16,1024]{2,1,0:T(8,128)(2,1)S(1)}, u32[]{:S(2)}, u32[]{:S(2)}) async-start(bf16[32,16,1024]{2,1,0:T(8,128)(2,1)} %stack.3), calls=%async_computation | async-start | bytes 2097152 | tf_op jit(solution)/shard_map/all_to_all | solution.py:86
  100.1 0.0 copy-done.4
  100.1 0.1 copy.69
  100.2 29.1 %all-to-all-done = bf16[32,16,1024]{2,1,0:T(8,128)(2,1)S(1)} async-done(((bf16[32,16,1024]{2,1,0:T(8,128)(2,1)}), bf16[32,16,1024]{2,1,0:T(8,128)(2,1)S(1)}, u32[]{:S(2)}, u32[]{:S(2)}) %all-to-all-start) | async-done | bytes 1048608 | tf_op jit(solution)/shard_map/all_to_all | solution.py:86
  129.4 0.1 fusion.42
  129.4 0.0 copy-done.2
  129.5 0.2 copy.47
  129.7 0.2 copy.44
  129.9 0.8 multiply_reduce_fusion
  130.7 1.3 fusion.15
  132.0 1.5 fusion.27
  133.5 31.7 %all-gather.4.cloned.1.call-done = bf16[2048,1024]{1,0:T(8,128)(2,1)} async-done(((bf16[64,1024]{1,0:T(8,128)(2,1)}), bf16[2048,1024]{1,0:T(8,128)(2,1)}) %all-gather.4.cloned.1.call-update) | async-done | bytes 4194320 | tf_op jit(solution)/shard_map/all_gather | solution.py:90
  165.2 26.3 %conditional.1 = ((f32[4,64,8]{2,1,0:T(8,128)S(1)}, f32[4,64,8,128]{3,2,1,0:T(8,128)S(1)})) conditional(s32[]{:T(128)} %convert_element_type.57, (f32[4,64,8]{2,1,0:T(8,128)S(1)}, f32[4,64,8,128]{3,2,1,0:T(8,128)S(1)}) %tuple.15, (s32[]{:T(128)}, s32[64,1]{0,1:T(1,128)S(1)}, s32[64,2048]{1,0:T(8,128)S(1)}, bf16[2048,1024]{1,0:T(8,128)(2,1)}, ...), branch_computations={%region_4.5_spmd, %region_5.8_spmd} | conditional | flops 2194280448 | bytes 75088664 | solution.py:93
  165.3 0.1 broadcast_compare_fusion
  165.4 6.5 %copy.52 = bf16[2048,1024]{0,1:T(8,128)(2,1)} copy(bf16[2048,1024]{1,0:T(8,128)(2,1)} %get-tuple-element.66) | data formatting | bytes 8388608 | tf_op jit(solution)/shard_map
  171.9 4.0 %fusion.41 = (bf16[2048,512]{0,1:T(8,128)(2,1)}, bf16[2048,512]{0,1:T(8,128)(2,1)S(1)}) fusion(bf16[2048,1024]{0,1:T(8,128)(2,1)} %copy.52), kind=kLoop, calls=%fused_computation.55 | loop fusion | bytes 8388608 | tf_op jit(solution)/shard_map/cond/branch_1_fun/slice | solution.py:54
  176.0 3.9 %select_reduce_fusion = (f32[4,64,8]{2,1,0:T(8,128)S(1)}, f32[4,64,8,2048]{3,2,1,0:T(8,128)S(1)}) fusion(pred[64,2048]{1,0:T(8,128)(4,1)S(1)} %broadcast_compare_fusion, bf16[2048,4,128,1]{0,2,3,1:T(8,128)(2,1)S(1)} %bitcast.63, bf16[64,4,8,128]{3,2,1,0:T(8,128)(2,1)S(1)} %get-tuple-element.67), kind=kOutput, calls=%fused_computation.2 | convolution fusion | flops 1086322688 | bytes 19537920 | tf_op jit(solution)/shard_map/cond/branch_1_fun/rgjd,ngd->grjn/dot_general | solution.py:56
  179.8 5.0 %fusion.1 = f32[4,64,8]{2,1,0:T(8,128)S(1)} fusion(f32[4,64,8,2048]{3,2,1,0:T(8,128)S(1)} %get-tuple-element.76, f32[4,64,8]{2,1,0:T(8,128)S(1)} %max.2, pred[64,2048]{1,0:T(8,128)(4,1)S(1)} %broadcast_compare_fusion), kind=kLoop, calls=%fused_computation.4 | loop fusion | flops 16775168 | bytes 16924672 | tf_op jit(solution)/shard_map/cond/branch_1_fun/reduce_sum | solution.py:63
  184.9 0.1 multiply_add_fusion
  185.0 6.5 %fusion.5 = f32[4,64,8,128]{3,2,1,0:T(8,128)S(1)} fusion(bf16[2048,4,128,1]{0,2,3,1:T(8,128)(2,1)} %bitcast.69, f32[4,64,8,2048]{3,2,1,0:T(8,128)S(1)} %get-tuple-element.76, f32[4,64,8]{2,1,0:T(8,128)S(1)} %max.2, pred[64,2048]{1,0:T(8,128)(4,1)S(1)} %broadcast_compare_fusion, f32[4,64,8,128]{3,2,1,0:T(8,128)S(1)} %get-tuple-element.32, ...), kind=kOutput, calls=%fused_computation.7 | convolution fusion | flops 1091043328 | bytes 21118976 | tf_op jit(solution)/shard_map/cond/branch_1_fun/grjn,ngd->grjd/dot_general | solution.py:64
  191.5 0.0 copy-start.1
  191.5 0.0 copy-start.3
  191.5 0.3 divide_bitcast_fusion
  191.9 0.1 copy.54
  192.0 0.2 reshape.133
  192.2 0.3 copy-done.1
  192.6 0.1 fusion.32
  192.7 3.1 %collective-permute-start = (bf16[1,64,4096]{2,1,0:T(8,128)(2,1)S(1)}, bf16[1,64,4096]{2,1,0:T(8,128)(2,1)S(1)}, u32[]{:S(2)}, u32[]{:S(2)}) collective-permute-start(bf16[1,64,4096]{2,1,0:T(8,128)(2,1)S(1)} %fusion.32), channel_id=1, source_target_pairs={{480,0},{0,32},{32,64},{64,96},{96,128},{128,160},{160,192},{192,2... | collective-permute-start | bytes 1572872 | tf_op jit(solution)/shard_map/ppermute | solution.py:15
  195.8 0.0 copy-done.3
  195.8 0.1 copy.51
  195.9 0.7 convert_element_type.67
  196.6 51.5 %collective-permute-done = bf16[1,64,4096]{2,1,0:T(8,128)(2,1)S(1)} collective-permute-done((bf16[1,64,4096]{2,1,0:T(8,128)(2,1)S(1)}, bf16[1,64,4096]{2,1,0:T(8,128)(2,1)S(1)}, u32[]{:S(2)}, u32[]{:S(2)}) %collective-permute-start) | collective-permute-done | bytes 524320 | tf_op jit(solution)/shard_map/ppermute | solution.py:15
  248.1 0.8 copy.90
  (10 shorter events, 0.1 us)
Async XLA Ops:
  7.2 5.2 %copy-start = (bf16[1,64,4096]{2,1,0:T(8,128)(2,1)S(1)}, bf16[1,64,4096]{2,1,0:T(8,128)(2,1)}, u32[]{:S(2)}) copy-start(bf16[1,64,4096]{2,1,0:T(8,128)(2,1)} %param.9) | copy-start | bytes 1572868
  7.2 74.9 %all-gather.6.cloned.1.call-start = ((), (), s32[]{:S(2)}) async-start(), calls=%async_computation.2 | async-start | bytes 5406720 | tf_op jit(solution)/shard_map/all_gather | solution.py:76
  7.9 157.3 %all-gather.4.cloned.1.call-start = ((), (), s32[]{:S(2)}) async-start(), calls=%async_computation.1 | async-start | bytes 4325376 | tf_op jit(solution)/shard_map/all_gather | solution.py:90
  88.5 3.7 %copy-start.5 = (bf16[1,16,1024]{2,1,0:T(8,128)(2,1)S(1)}, bf16[1,16,1024]{2,1,0:T(8,128)(2,1)}, u32[]{:S(2)}) copy-start(bf16[1,16,1024]{2,1,0:T(8,128)(2,1)} %param.12) | copy-start | bytes 98308
  88.5 11.6 %copy-start.4 = (bf16[1,64,4096]{2,1,0:T(8,128)(2,1)S(1)}, bf16[1,64,4096]{2,1,0:T(8,128)(2,1)}, u32[]{:S(2)}) copy-start(bf16[1,64,4096]{2,1,0:T(8,128)(2,1)} %param.11) | copy-start | bytes 1572868
  91.5 37.9 %copy-start.2 = (bf16[64,8,128]{2,0,1:T(8,128)(2,1)}, bf16[64,8,128]{2,0,1:T(8,128)(2,1)S(1)}, u32[]{:S(2)}) copy-start(bf16[64,8,128]{2,0,1:T(8,128)(2,1)S(1)} %reduce_sum.38) | copy-start | bytes 393220
  93.3 36.0 %all-to-all-start = ((bf16[32,16,1024]{2,1,0:T(8,128)(2,1)}), bf16[32,16,1024]{2,1,0:T(8,128)(2,1)S(1)}, u32[]{:S(2)}, u32[]{:S(2)}) async-start(bf16[32,16,1024]{2,1,0:T(8,128)(2,1)} %stack.3), calls=%async_computation | async-start | bytes 2097152 | tf_op jit(solution)/shard_map/all_to_all | solution.py:86
  191.5 1.0 copy-start.1
  191.5 4.2 %copy-start.3 = (bf16[64,8,128]{2,0,1:T(8,128)(2,1)S(1)}, bf16[64,8,128]{2,0,1:T(8,128)(2,1)}, u32[]{:S(2)}) copy-start(bf16[64,8,128]{2,0,1:T(8,128)(2,1)} %copy-done.2) | copy-start | bytes 393220
  192.7 55.4 %collective-permute-start = (bf16[1,64,4096]{2,1,0:T(8,128)(2,1)S(1)}, bf16[1,64,4096]{2,1,0:T(8,128)(2,1)S(1)}, u32[]{:S(2)}, u32[]{:S(2)}) collective-permute-start(bf16[1,64,4096]{2,1,0:T(8,128)(2,1)S(1)} %fusion.32), channel_id=1, source_target_pairs={{480,0},{0,32},{32,64},{64,96},{96,128},{128,160},{160,192},{192,2... | collective-permute-start | bytes 1572872 | tf_op jit(solution)/shard_map/ppermute | solution.py:15
Sparse Core Ops, SparseCore 0:
  10.1 71.9 all-gather.5
  92.4 72.7 all-gather.3
